TPU v7x, 256 devices: a whole 4x4x8 slice. The times are simulated.
256 devices in a mesh: dp: 4 (over z_lo, core), cp: 16 (over y, z_hi), tp: 4 (over x).
Axes of the slice: x: 4, y: 4, z: 8 (z_hi: 4, z_lo: 2; z = z_hi * 2 + z_lo), core: 2. Of those that a mesh axis runs over, the one named last changes fastest.
Arguments:
- hidden: bfloat16 [4, 2048, 8192], P('dp', 'cp'), may hold values from -6 to 6
- query: bfloat16 [4, 2048, 8192], P('dp', 'cp', 'tp'), may hold values from -360 to 360
- grad_out: bfloat16 [4, 2048, 8192], P('dp', 'cp', 'tp'), may hold values from -6 to 6
- k_weight: bfloat16 [8192, 1024], P('dp', 'tp'), may hold values from -0.0625 to 0.0625
- v_weight: bfloat16 [8192, 1024], P('dp', 'tp'), may hold values from -0.0625 to 0.0625
- doc_starts: int32 [4, 4], P('dp'), may hold values from 0 to 2047, as said below
Outputs:
- attn_out: bfloat16 [4, 2048, 8192], P('dp', 'cp', 'tp')
- query_grad: bfloat16 [4, 2048, 8192], P('dp', 'cp', 'tp')
- k_weight_grad: float32 [8192, 1024], P(('dp', 'cp'), 'tp')
- v_weight_grad: float32 [8192, 1024], P(('dp', 'cp'), 'tp')
Inputs may be any that keep to these rules, and one draw needn't show every extreme that they name: `doc_starts`: in each sequence the starts strictly increase and the first is 0.
All inputs are finite; a program needn't handle non-finite values.
Results may differ from a plain program's by a relative error of at most 0.04.
The roundings to bfloat16 on the way count: a program that leaves them out, or rounds other values in their place, can miss the bound.
Values may be sent and summed in bfloat16 or wider, within the bound.
No kernel may reach another device: no remote copies, remote signals or barrier semaphores. Data moves between devices by JAX's collectives and lax.ppermute only.
A program may use at most 128 MiB of HBM per device.

v0:
```python
import math
import jax
import jax.numpy as jnp
from jax import lax
from jax.sharding import PartitionSpec as P

DH = 128
NEG_BIG = -1e30


def place(rows, tok_rows, seq_rows):
    stretch = rows // tok_rows
    within = rows % tok_rows
    half_rows = tok_rows // 2
    return jnp.where(
        within < half_rows,
        stretch * half_rows + within,
        seq_rows - (stretch + 1) * half_rows + within - half_rows,
    )


def doc_index(positions, starts):
    return jnp.sum((starts[None, :] <= positions[:, None]).astype(jnp.int32), axis=1) - 1


def sweep(update, initial, all_keys, all_vals, span):

    def step_fn(block_index, running):
        first_row = block_index * span
        pieces = (
            lax.dynamic_slice_in_dim(all_keys, first_row, span, 0),
            lax.dynamic_slice_in_dim(all_vals, first_row, span, 0),
        )
        return update(running, pieces, first_row)

    return lax.fori_loop(0, all_keys.shape[0] // span, step_fn, initial)


def on_device(hidden, query, grad_out, k_weight, v_weight, doc_starts):
    inputs = hidden[0]
    tok_rows = inputs.shape[0]
    cp_count = lax.axis_size("cp")
    seq_rows = tok_rows * cp_count
    score_scale = DH ** (-0.5)
    kv_width = k_weight.shape[1]
    kv_heads = kv_width // DH
    per_group = query.shape[2] // DH // kv_heads
    starts = doc_starts[0]
    own_rows = lax.axis_index("cp") * tok_rows + jnp.arange(tok_rows, dtype=jnp.int32)
    own_place = place(own_rows, tok_rows, seq_rows)
    own_doc = doc_index(own_place, starts)

    def allowed_pairs(first_row, piece_rows):
        key_place = place(first_row + jnp.arange(piece_rows, dtype=jnp.int32), tok_rows, seq_rows)
        key_doc = doc_index(key_place, starts)
        return (key_place[None, :] <= own_place[:, None]) & (key_doc[None, :] == own_doc[:, None])

    pieces = (
        lax.all_gather(k_weight, "dp", axis=0, tiled=True),
        lax.all_gather(v_weight, "dp", axis=0, tiled=True),
    )
    columns = inputs
    key_sums = jnp.dot(columns, pieces[0], preferred_element_type=jnp.float32)
    value_sums = jnp.dot(columns, pieces[1], preferred_element_type=jnp.float32)
    keys = key_sums.astype(jnp.bfloat16)
    values = value_sums.astype(jnp.bfloat16)
    queries = query[0].reshape(tok_rows, kv_heads, per_group, DH)
    upstream = grad_out[0].reshape(tok_rows, kv_heads, per_group, DH)

    def totals_step(running, pieces, first_row):
        key_piece = pieces[0]
        piece_rows = key_piece.shape[0]
        allowed = allowed_pairs(first_row, piece_rows)
        top_score, denom = running
        key_heads = key_piece.reshape(piece_rows, kv_heads, DH)
        scores = (
            jnp.einsum("qgid,kgd->giqk", queries, key_heads, preferred_element_type=jnp.float32)
            * score_scale
        )
        scores = jnp.where(allowed, scores, NEG_BIG)
        fresh_top = jnp.maximum(top_score, jnp.max(scores, axis=-1))
        expos = jnp.where(allowed, jnp.exp(scores - fresh_top[..., None]), 0.0)
        denom = denom * jnp.exp(top_score - fresh_top) + jnp.sum(expos, axis=-1)
        return (fresh_top, denom)

    start_totals = (
        jnp.full((kv_heads, per_group, tok_rows), NEG_BIG, jnp.float32),
        jnp.zeros((kv_heads, per_group, tok_rows), jnp.float32),
    )
    span = tok_rows * math.gcd(cp_count, max(1, 512 // tok_rows))
    all_keys, all_vals = (
        lax.all_gather(keys, "cp", axis=0, tiled=True),
        lax.all_gather(values, "cp", axis=0, tiled=True),
    )
    top_score, denom = sweep(totals_step, start_totals, all_keys, all_vals, span)
    log_total = top_score + jnp.log(denom)

    def output_step(running, pieces, first_row):
        key_piece, value_piece = pieces
        piece_rows = key_piece.shape[0]
        allowed = allowed_pairs(first_row, piece_rows)
        key_heads = key_piece.reshape(piece_rows, kv_heads, DH)
        value_heads = value_piece.reshape(piece_rows, kv_heads, DH)
        scores = (
            jnp.einsum("qgid,kgd->giqk", queries, key_heads, preferred_element_type=jnp.float32)
            * score_scale
        )
        weights_bf = jnp.where(allowed, jnp.exp(scores - log_total[..., None]), 0.0).astype(
            jnp.bfloat16
        )
        return running + jnp.einsum(
            "giqk,kgd->qgid", weights_bf, value_heads, preferred_element_type=jnp.float32
        )

    start_output = jnp.zeros((tok_rows, kv_heads, per_group, DH), jnp.float32)
    accum = sweep(output_step, start_output, all_keys, all_vals, span)
    out_rows = accum.astype(jnp.bfloat16)
    delta = jnp.transpose(
        jnp.sum(upstream.astype(jnp.float32) * out_rows.astype(jnp.float32), axis=-1), (1, 2, 0)
    )

    def backward(running, pieces, first_row):
        key_piece, value_piece = pieces
        piece_rows = key_piece.shape[0]
        allowed = allowed_pairs(first_row, piece_rows)
        query_acc, key_term, value_term = running
        key_heads = key_piece.reshape(piece_rows, kv_heads, DH)
        value_heads = value_piece.reshape(piece_rows, kv_heads, DH)
        scores = (
            jnp.einsum("qgid,kgd->giqk", queries, key_heads, preferred_element_type=jnp.float32)
            * score_scale
        )
        weights = jnp.where(allowed, jnp.exp(scores - log_total[..., None]), 0.0)
        weights_bf = weights.astype(jnp.bfloat16)
        prob_grads = jnp.einsum(
            "qgid,kgd->giqk", upstream, value_heads, preferred_element_type=jnp.float32
        )
        score_grads = (weights * (prob_grads - delta[..., None])).astype(jnp.bfloat16)
        query_acc = (
            query_acc
            + jnp.einsum(
                "giqk,kgd->qgid", score_grads, key_heads, preferred_element_type=jnp.float32
            )
            * score_scale
        )
        key_piece_grad = (
            jnp.einsum("giqk,qgid->kgd", score_grads, queries, preferred_element_type=jnp.float32)
            * score_scale
        )
        value_piece_grad = jnp.einsum(
            "giqk,qgid->kgd", weights_bf, upstream, preferred_element_type=jnp.float32
        )
        key_term = lax.dynamic_update_slice_in_dim(
            key_term, key_piece_grad.reshape(piece_rows, kv_width), first_row, 0
        )
        value_term = lax.dynamic_update_slice_in_dim(
            value_term, value_piece_grad.reshape(piece_rows, kv_width), first_row, 0
        )
        return (query_acc, key_term, value_term)

    start_backward = (
        jnp.zeros((tok_rows, kv_heads, per_group, DH), jnp.float32),
        jnp.zeros((seq_rows, kv_width), jnp.float32),
        jnp.zeros((seq_rows, kv_width), jnp.float32),
    )
    query_acc, key_term, value_term = sweep(backward, start_backward, all_keys, all_vals, span)
    key_sum, value_sum = (
        lax.psum_scatter(
            key_term.astype(jnp.bfloat16), "cp", scatter_dimension=0, tiled=True
        ).astype(jnp.float32),
        lax.psum_scatter(
            value_term.astype(jnp.bfloat16), "cp", scatter_dimension=0, tiled=True
        ).astype(jnp.float32),
    )
    both_grads = jnp.concatenate(
        [key_sum.astype(jnp.bfloat16), value_sum.astype(jnp.bfloat16)], axis=1
    )
    columns = inputs
    result = lax.psum_scatter(
        jnp.dot(columns.T, both_grads, preferred_element_type=jnp.float32),
        ("dp", "cp"),
        scatter_dimension=0,
        tiled=True,
    )
    attn_rows = out_rows.reshape(1, tok_rows, kv_heads * per_group * DH)
    query_rows = query_acc.astype(jnp.bfloat16).reshape(1, tok_rows, kv_heads * per_group * DH)
    return (attn_rows, query_rows, result[:, :kv_width], result[:, kv_width:])


def solution(mesh):
    placed = (
        P("dp", "cp", None),
        P("dp", "cp", "tp"),
        P("dp", "cp", "tp"),
        P("dp", "tp"),
        P("dp", "tp"),
        P("dp", None),
    )
    return jax.shard_map(
        on_device,
        mesh=mesh,
        in_specs=placed,
        out_specs=(
            P("dp", "cp", "tp"),
            P("dp", "cp", "tp"),
            P(("dp", "cp"), "tp"),
            P(("dp", "cp"), "tp"),
        ),
        check_vma=False,
    )
```

profile of v0, /device:TPU:36, one launch (start us, length us, event | category | flops | bytes accessed | tf_op | source)
XLA Modules:
  0.0 896.1 jit_solution(16444612808211321503)
XLA Ops:
  8.7 51.0 %all-gather.9.cloned.1.call-done = bf16[8192,256]{1,0:T(8,128)(2,1)} async-done(((bf16[2048,256]{1,0:T(8,128)(2,1)}), bf16[8192,256]{1,0:T(8,128)(2,1)}) %all-gather.9.cloned.1.call-update) | async-done | bytes 4194320 | tf_op jit(solution)/shard_map/all_gather | solution.py:59
  59.8 3.5 fusion.43
  64.0 2.0 copy.106
  66.2 44.9 %all-gather.5.cloned.1.call-done = bf16[8192,256]{1,0:T(8,128)(2,1)} async-done(((bf16[2048,256]{1,0:T(8,128)(2,1)}), bf16[8192,256]{1,0:T(8,128)(2,1)}) %all-gather.5.cloned.1.call-update) | async-done | bytes 4194320 | tf_op jit(solution)/shard_map/all_gather | solution.py:60
  111.0 3.5 fusion.40
  114.6 53.1 %all-gather.11.cloned.1.call-done = bf16[2048,256]{1,0:T(8,128)(2,1)} async-done(((bf16[128,256]{1,0:T(8,128)(2,1)}), bf16[2048,256]{1,0:T(8,128)(2,1)}) %all-gather.11.cloned.1.call-update) | async-done | bytes 1048592 | tf_op jit(solution)/shard_map/all_gather | solution.py:92
  167.7 2.3 copy.103
  170.0 12.9 %while.57 = (s32[]{:T(128)}, f32[2,8,128]{2,1,0:T(8,128)S(1)}, f32[2,8,128]{2,1,0:T(8,128)S(1)}, s32[1,4]{1,0:T(1,128)S(1)}, s32[128]{0:T(128)S(1)}, /*index=5*/...) while((s32[]{:T(128)}, f32[2,8,128]{2,1,0:T(8,128)S(1)}, ...), condition=%wide.region_5.6_spmd.clone, body=%wide.region_1.5_spmd.clone.sunk | while | flops 277055616 | bytes 10018514 | solution.py:36
  182.9 38.2 %all-gather.7.cloned.1.call-done = bf16[2048,256]{1,0:T(8,128)(2,1)} async-done(((bf16[128,256]{1,0:T(8,128)(2,1)}), bf16[2048,256]{1,0:T(8,128)(2,1)}) %all-gather.7.cloned.1.call-update) | async-done | bytes 1048592 | tf_op jit(solution)/shard_map/all_gather | solution.py:93
  221.2 2.3 copy.102
  223.5 22.7 %while.58 = (s32[]{:T(128)}, f32[128,2,8,128]{0,3,2,1:T(8,128)}, bf16[2048,256]{0,1:T(8,128)(2,1)}, s32[1,4]{1,0:T(1,128)S(1)}, s32[128]{0:T(128)S(1)}, /*index=...) while((s32[]{:T(128)}, f32[128,2,8,128]{0,3,2,1:T(8,128)}, ...), condition=%wide.region_8.9_spmd.clone, body=%wide.region_6.8_spmd.clone.sunk | while | flops 541810816 | bytes 4349657 | solution.py:36
  225.6 3.3 fusion.98
  229.2 1.8 constant_dynamic-slice_fusion.10
  231.0 3.6 fusion.98
  236.7 3.6 fusion.98
  242.5 3.6 fusion.98
  246.1 2.4 multiply_reduce_fusion
  250.8 32.6 %while.59 = (s32[]{:T(128)}, f32[128,2,8,128]{0,3,2,1:T(8,128)}, bf16[2048,256]{0,1:T(8,128)(2,1)}, bf16[2048,256]{0,1:T(8,128)(2,1)}, bf16[2048,256]{0,1:T(8,12...) while((s32[]{:T(128)}, f32[128,2,8,128]{0,3,2,1:T(8,128)}, ...), condition=%wide.region_12.13_spmd.clone, body=%wide.region_10.12_spmd.clone.sunk | while | flops 1353932928 | bytes 35102520 | solution.py:36
  283.4 2.3 copy.138
  285.7 2.3 copy.136
  288.3 83.3 %reduce-scatter.12.cloned.1.call-done = bf16[128,256]{1,0:T(8,128)(2,1)} async-done(((bf16[2048,256]{1,0:T(8,128)(2,1)}), bf16[128,256]{1,0:T(8,128)(2,1)}) %reduce-scatter.12.cloned.1.call-update) | async-done | bytes 65552
  372.5 87.5 %reduce-scatter.10.cloned.1.call-done = bf16[128,256]{1,0:T(8,128)(2,1)} async-done(((bf16[2048,256]{1,0:T(8,128)(2,1)}), bf16[128,256]{1,0:T(8,128)(2,1)}) %reduce-scatter.10.cloned.1.call-update) | async-done | bytes 65552
  461.0 8.1 convolution_bitcast_fusion.1
  473.4 413.3 %reduce-scatter.8.cloned.1.call-done = f32[128,512]{0,1:T(8,128)} async-done(((f32[8192,512]{0,1:T(8,128)}), f32[128,512]{0,1:T(8,128)}) %reduce-scatter.8.cloned.1.call-update) | async-done | bytes 262160 | tf_op jit(solution)/shard_map/reduce_scatter | solution.py:179
  (179 shorter events, 65.2 us)
Async XLA Ops:
  7.2 52.6 %copy-start = (bf16[1,128,8192]{2,1,0:T(8,128)(2,1)S(1)}, bf16[1,128,8192]{2,1,0:T(8,128)(2,1)}, u32[]{:S(2)}) copy-start(bf16[1,128,8192]{2,1,0:T(8,128)(2,1)} %param.12) | copy-start | bytes 6291460
  7.2 56.2 %copy-start.5 = (bf16[1,128,2048]{2,1,0:T(8,128)(2,1)S(1)}, bf16[1,128,2048]{2,1,0:T(8,128)(2,1)}, u32[]{:S(2)}) copy-start(bf16[1,128,2048]{2,1,0:T(8,128)(2,1)} %param.13) | copy-start | bytes 1572868
  7.2 52.6 %all-gather.9.cloned.1.call-start = ((), (), s32[]{:S(2)}) async-start(), calls=%async_computation.5 | async-start | bytes 5242880 | tf_op jit(solution)/shard_map/all_gather | solution.py:59
  7.9 103.1 %all-gather.5.cloned.1.call-start = ((), (), s32[]{:S(2)}) async-start(), calls=%async_computation.3 | async-start | bytes 5242880 | tf_op jit(solution)/shard_map/all_gather | solution.py:60
  8.7 57.4 %copy-start.6 = (s32[1,4]{1,0:T(1,128)S(1)}, s32[1,4]{1,0:T(1,128)}, u32[]{:S(2)}) copy-start(s32[1,4]{1,0:T(1,128)} %param.17) | copy-start | bytes 52
  8.7 159.0 %all-gather.11.cloned.1.call-start = ((), (), s32[]{:S(2)}) async-start(), calls=%async_computation.6 | async-start | bytes 1114112 | tf_op jit(solution)/shard_map/all_gather | solution.py:92
  63.3 157.9 %all-gather.7.cloned.1.call-start = ((), (), s32[]{:S(2)}) async-start(), calls=%async_computation.4 | async-start | bytes 1114112 | tf_op jit(solution)/shard_map/all_gather | solution.py:93
  114.6 257.0 %reduce-scatter.12.cloned.1.call-start = ((), (), s32[]{:S(2)}) async-start(), calls=%async_computation.9 | async-start | bytes 1114112
  246.1 4.6 copy-start.3
  254.8 2.3 copy-start.1
  257.7 1.2 copy-start.2
  262.9 2.3 copy-start.1
  265.9 1.2 copy-start.2
  271.1 2.3 copy-start.1
  274.1 1.2 copy-start.2
  279.3 2.3 copy-start.1
  282.2 1.2 copy-start.2
  285.7 174.3 %reduce-scatter.10.cloned.1.call-start = ((), (), s32[]{:S(2)}) async-start(), calls=%async_computation.8 | async-start | bytes 1114112
  288.1 598.7 %reduce-scatter.8.cloned.1.call-start = ((), (), s32[]{:S(2)}) async-start(), calls=%async_computation.7 | async-start | bytes 17039360 | tf_op jit(solution)/shard_map/reduce_scatter | solution.py:179
  469.1 1.0 copy-start.4
Sparse Core Ops, SparseCore 0:
  9.8 49.9 all-gather.8
  61.6 49.4 all-gather.4
  114.0 53.6 all-gather.10
  170.6 50.5 all-gather.6
  285.8 85.6 reduce-scatter.11
  374.9 85.0 reduce-scatter.9
  469.2 417.5 reduce-scatter.7
where the time goes:
time: 897 us; the launch traced here: 896 us
  waiting for transfers between devices  773 us (86%)
  matrix products  51.1 us (6%)
  local copies, waits for them, and re-layouts  45 us (5%)
  between operations  14.3 us (2%)
  other arithmetic  11.9 us (1%)
    reduce_scatter x1, waiting for transfers between devices, on_device(): lax.psum_scatter(jnp.dot(columns.T, both_grads, preferred_element_type=jn...  413 us
    unnamed x9, waiting for transfers between devices  172 us
    all_gather x1, waiting for transfers between devices, on_device(): lax.all_gather(keys, 'cp', axis=0, tiled=True)  53.1 us
    all_gather x1, waiting for transfers between devices, on_device(): lax.all_gather(k_weight, 'dp', axis=0, tiled=True)  51 us
    all_gather x1, waiting for transfers between devices, on_device(): lax.all_gather(v_weight, 'dp', axis=0, tiled=True)  44.9 us
    all_gather x1, waiting for transfers between devices, on_device(): lax.all_gather(values, 'cp', axis=0, tiled=True)  38.2 us
  transfers between devices with their start and end apart: 7, of which 7 were waited for; matrix products, arithmetic and copies ran while one was open for 3% of the time, Pallas kernels for 0%

commit v1 on v0

--- a/solution.py
+++ b/solution.py
@@ -56,7 +56,9 @@
         return (key_place[None, :] <= own_place[:, None]) & (key_doc[None, :] == own_doc[:, None])
 
     pieces = (
-        lax.all_gather(k_weight, "dp", axis=0, tiled=True),
+        jnp.concatenate(
+            lax.all_to_all(jnp.stack([k_weight] * lax.axis_size("dp")), "dp", 0, 0), axis=0
+        ),
         lax.all_gather(v_weight, "dp", axis=0, tiled=True),
     )
     columns = inputs

time: 897 us -> 879 us (0.980)
  waiting for transfers between devices: 773 us -> 746 us
    all_to_all x0 -> x1, waiting for transfers between devices: none -> 72.1 us  [on_device(): lax.all_to_all(jnp.stack([k_weight] * lax.axis_size('dp')), 'dp', 0, 0)]
    all_gather x1 -> x0, waiting for transfers between devices: 51 us -> none  [on_device(): lax.all_gather(k_weight, 'dp', axis=0, tiled=True)]
    all_gather x1, waiting for transfers between devices: 44.9 us -> 0.82 us  [on_device(): lax.all_gather(v_weight, 'dp', axis=0, tiled=True)]
    unnamed x9 -> x8, waiting for transfers between devices: 172 us -> 172 us
  transfers between devices with their start and end apart: 7 -> 7, of which waited for: 7 -> 7; matrix products, arithmetic and copies ran while one was open for 3% -> 4% of each run, Pallas kernels for 0% -> 0%
where the time goes in v1:
time: 879 us; the launch traced here: 878 us
  waiting for transfers between devices  746 us (85%)
  matrix products  51.1 us (6%)
  local copies, waits for them, and re-layouts  48.5 us (6%)
  between operations  14.2 us (2%)
  other arithmetic  11.9 us (1%)
    reduce_scatter x1, waiting for transfers between devices, on_device(): lax.psum_scatter(jnp.dot(columns.T, both_grads, preferred_element_type=jn...  408 us
    unnamed x8, waiting for transfers between devices  172 us
    all_to_all x1, waiting for transfers between devices, on_device(): lax.all_to_all(jnp.stack([k_weight] * lax.axis_size('dp')), 'dp', 0, 0)  72.1 us
    all_gather x1, waiting for transfers between devices, on_device(): lax.all_gather(keys, 'cp', axis=0, tiled=True)  55.1 us
    all_gather x1, waiting for transfers between devices, on_device(): lax.all_gather(values, 'cp', axis=0, tiled=True)  38.4 us
  transfers between devices with their start and end apart: 7, of which 7 were waited for; matrix products, arithmetic and copies ran while one was open for 4% of the time, Pallas kernels for 0%

profile of v1, /device:TPU:36, one launch (start us, length us, event | category | flops | bytes accessed | tf_op | source)
XLA Modules:
  0.0 878.0 jit_solution(5522082415263649437)
XLA Ops:
  7.2 3.6 stack.2
  10.8 4.9 all-to-all-start
  16.5 72.1 %all-to-all-done = bf16[4,2048,256]{2,1,0:T(8,128)(2,1)} async-done(((bf16[4,2048,256]{2,1,0:T(8,128)(2,1)}), bf16[4,2048,256]{2,1,0:T(8,128)(2,1)}, u32[]{:S(2)}, u32[]{:S(2)}) %all-to-all-start) | async-done | bytes 4194336 | tf_op jit(solution)/shard_map/all_to_all | solution.py:60
  88.6 3.5 fusion.43
  92.8 2.0 copy.106
  95.8 3.5 fusion.40
  99.4 55.1 %all-gather.8.cloned.1.call-done = bf16[2048,256]{1,0:T(8,128)(2,1)} async-done(((bf16[128,256]{1,0:T(8,128)(2,1)}), bf16[2048,256]{1,0:T(8,128)(2,1)}) %all-gather.8.cloned.1.call-update) | async-done | bytes 1048592 | tf_op jit(solution)/shard_map/all_gather | solution.py:94
  154.5 2.3 copy.103
  156.7 13.0 %while.57 = (s32[]{:T(128)}, f32[2,8,128]{2,1,0:T(8,128)S(1)}, f32[2,8,128]{2,1,0:T(8,128)S(1)}, s32[1,4]{1,0:T(1,128)S(1)}, s32[128]{0:T(128)S(1)}, /*index=5*/...) while((s32[]{:T(128)}, f32[2,8,128]{2,1,0:T(8,128)S(1)}, ...), condition=%wide.region_5.6_spmd.clone, body=%wide.region_1.5_spmd.clone.sunk | while | flops 277055616 | bytes 10018514 | solution.py:36
  169.7 38.4 %all-gather.6.cloned.1.call-done = bf16[2048,256]{1,0:T(8,128)(2,1)} async-done(((bf16[128,256]{1,0:T(8,128)(2,1)}), bf16[2048,256]{1,0:T(8,128)(2,1)}) %all-gather.6.cloned.1.call-update) | async-done | bytes 1048592 | tf_op jit(solution)/shard_map/all_gather | solution.py:95
  208.1 2.3 copy.102
  210.4 22.7 %while.58 = (s32[]{:T(128)}, f32[128,2,8,128]{0,3,2,1:T(8,128)}, bf16[2048,256]{0,1:T(8,128)(2,1)}, s32[1,4]{1,0:T(1,128)S(1)}, s32[128]{0:T(128)S(1)}, /*index=...) while((s32[]{:T(128)}, f32[128,2,8,128]{0,3,2,1:T(8,128)}, ...), condition=%wide.region_8.9_spmd.clone, body=%wide.region_6.8_spmd.clone.sunk | while | flops 541810816 | bytes 4349657 | solution.py:36
  212.5 3.3 fusion.98
  217.9 3.7 fusion.98
  223.7 3.7 fusion.98
  229.5 3.7 fusion.98
  233.1 2.4 multiply_reduce_fusion
  237.7 32.6 %while.59 = (s32[]{:T(128)}, f32[128,2,8,128]{0,3,2,1:T(8,128)}, bf16[2048,256]{0,1:T(8,128)(2,1)}, bf16[2048,256]{0,1:T(8,128)(2,1)}, bf16[2048,256]{0,1:T(8,12...) while((s32[]{:T(128)}, f32[128,2,8,128]{0,3,2,1:T(8,128)}, ...), condition=%wide.region_12.13_spmd.clone, body=%wide.region_10.12_spmd.clone.sunk | while | flops 1353932928 | bytes 35102520 | solution.py:36
  270.3 2.3 copy.138
  272.7 2.3 copy.136
  275.2 83.2 %reduce-scatter.12.cloned.1.call-done = bf16[128,256]{1,0:T(8,128)(2,1)} async-done(((bf16[2048,256]{1,0:T(8,128)(2,1)}), bf16[128,256]{1,0:T(8,128)(2,1)}) %reduce-scatter.12.cloned.1.call-update) | async-done | bytes 65552
  359.4 87.5 %reduce-scatter.10.cloned.1.call-done = bf16[128,256]{1,0:T(8,128)(2,1)} async-done(((bf16[2048,256]{1,0:T(8,128)(2,1)}), bf16[128,256]{1,0:T(8,128)(2,1)}) %reduce-scatter.10.cloned.1.call-update) | async-done | bytes 65552
  447.8 8.1 convolution_bitcast_fusion.1
  460.3 408.3 %reduce-scatter.8.cloned.1.call-done = f32[128,512]{0,1:T(8,128)} async-done(((f32[8192,512]{0,1:T(8,128)}), f32[128,512]{0,1:T(8,128)}) %reduce-scatter.8.cloned.1.call-update) | async-done | bytes 262160 | tf_op jit(solution)/shard_map/reduce_scatter | solution.py:181
  (179 shorter events, 67.1 us)
Async XLA Ops:
  7.2 81.4 %copy-start = (bf16[1,128,8192]{2,1,0:T(8,128)(2,1)S(1)}, bf16[1,128,8192]{2,1,0:T(8,128)(2,1)}, u32[]{:S(2)}) copy-start(bf16[1,128,8192]{2,1,0:T(8,128)(2,1)} %param.12) | copy-start | bytes 6291460
  10.8 77.8 %all-to-all-start = ((bf16[4,2048,256]{2,1,0:T(8,128)(2,1)}), bf16[4,2048,256]{2,1,0:T(8,128)(2,1)}, u32[]{:S(2)}, u32[]{:S(2)}) async-start(bf16[4,2048,256]{2,1,0:T(8,128)(2,1)} %stack.2), calls=%async_computation | async-start | bytes 8388608 | tf_op jit(solution)/shard_map/all_to_all | solution.py:60
  15.7 76.6 %copy-start.5 = (bf16[1,128,2048]{2,1,0:T(8,128)(2,1)S(1)}, bf16[1,128,2048]{2,1,0:T(8,128)(2,1)}, u32[]{:S(2)}) copy-start(bf16[1,128,2048]{2,1,0:T(8,128)(2,1)} %param.13) | copy-start | bytes 1572868
  15.7 80.1 %all-gather.4.cloned.1.call-start = ((), (), s32[]{:S(2)}) async-start(), calls=%async_computation.4 | async-start | bytes 5242880 | tf_op jit(solution)/shard_map/all_gather | solution.py:62
  16.4 138.1 %all-gather.8.cloned.1.call-start = ((), (), s32[]{:S(2)}) async-start(), calls=%async_computation.6 | async-start | bytes 1114112 | tf_op jit(solution)/shard_map/all_gather | solution.py:94
  88.6 6.3 copy-start.6
  92.1 116.0 %all-gather.6.cloned.1.call-start = ((), (), s32[]{:S(2)}) async-start(), calls=%async_computation.5 | async-start | bytes 1114112 | tf_op jit(solution)/shard_map/all_gather | solution.py:95
  99.4 259.1 %reduce-scatter.12.cloned.1.call-start = ((), (), s32[]{:S(2)}) async-start(), calls=%async_computation.9 | async-start | bytes 1114112
  233.1 4.6 copy-start.3
  241.7 2.3 copy-start.1
  244.7 1.2 copy-start.2
  249.9 2.3 copy-start.1
  252.8 1.2 copy-start.2
  258.0 2.3 copy-start.1
  261.0 1.2 copy-start.2
  266.2 2.3 copy-start.1
  269.1 1.2 copy-start.2
  272.6 174.2 %reduce-scatter.10.cloned.1.call-start = ((), (), s32[]{:S(2)}) async-start(), calls=%async_computation.8 | async-start | bytes 1114112
  275.0 593.6 %reduce-scatter.8.cloned.1.call-start = ((), (), s32[]{:S(2)}) async-start(), calls=%async_computation.7 | async-start | bytes 17039360 | tf_op jit(solution)/shard_map/reduce_scatter | solution.py:181
  455.9 1.0 copy-start.4
Sparse Core Ops, SparseCore 0:
  18.3 77.4 all-gather.3
  98.8 55.6 all-gather.7
  157.5 50.5 all-gather.5
  272.8 85.6 reduce-scatter.11
  361.8 85.0 reduce-scatter.9
  456.0 412.5 reduce-scatter.7
